TPU v7x, 128 devices: a whole 4x4x4 slice. The times are simulated.
128 devices in a mesh: dp: 16 (over x, y), feat: 8 (over z, core).
Axes of the slice: x: 4, y: 4, z: 4, core: 2. Of those that a mesh axis runs over, the one named last changes fastest.
Arguments:
- images: bfloat16 [8192, 3072], P(('dp', 'feat')), may hold values from -6 to 6
- labels: int32 [8192], P('dp'), may hold values from 0 to 999
- predictions: float32 [8192, 1000], P('dp'), may hold values from -2 to 2
- filters: bfloat16 [75, 1024], P(None, 'feat'), may hold values from -0.75 to 0.75
- biases: float32 [1024], P('feat'), may hold values from -3 to 3
Outputs:
- weights: float32 [4096, 1000], P('feat')
- new_residual: float32 [8192, 1000], P(('dp', 'feat'))
All inputs are finite; a program needn't handle non-finite values.
Results may differ from a plain program's by a relative error of at most 0.007.
The roundings to bfloat16 on the way count: a program that leaves them out, or rounds other values in their place, can miss the bound.
Values may be sent and summed in bfloat16 or wider, within the bound.
No kernel may reach another device: no remote copies, remote signals or barrier semaphores. Data moves between devices by JAX's collectives and lax.ppermute only.
A program may use at most 192 MiB of HBM per device.

v0:
```python
import math
import jax
import jax.numpy as jnp
from jax import lax
from jax.sharding import PartitionSpec as P

SIDE = 32
CHAN = 3
KSIZE = 5


def chol_solve(factor, rhs):
    middle = lax.linalg.triangular_solve(factor, rhs, left_side=True, lower=True, transpose_a=False)
    return lax.linalg.triangular_solve(factor, middle, left_side=True, lower=True, transpose_a=True)


def split_parts(values):
    upper = values.astype(jnp.bfloat16)
    lower = (values - upper.astype(jnp.float32)).astype(jnp.bfloat16)
    return (upper, lower)


def left_product(feats, other):
    return lax.dot_general(
        feats, other, (((0,), (0,)), ((), ())), preferred_element_type=jnp.float32
    )


def conv_pool(imgs, kernel, offsets):
    count = imgs.shape[0]
    filt_count = kernel.shape[3]
    pics = imgs.reshape(count, SIDE, SIDE, CHAN)
    response = lax.conv_general_dilated(
        pics,
        kernel,
        (1, 1),
        "VALID",
        dimension_numbers=("NHWC", "HWIO", "NHWC"),
        preferred_element_type=jnp.float32,
    )
    response = jnp.maximum(response + offsets, 0.0)
    half = (SIDE - KSIZE + 1) // 2
    pooled = response.reshape(count, 2, half, 2, half, filt_count).mean(axis=(2, 4))
    return jnp.transpose(pooled, (0, 3, 1, 2)).reshape(count, 4 * filt_count).astype(jnp.bfloat16)


def shards(images, labels, predictions, filters, biases):
    filt_count = filters.shape[1]
    kernel = filters.reshape(KSIZE, KSIZE, CHAN, filt_count)
    share = images.shape[0]
    total_images = share * lax.axis_size("feat") * lax.axis_size("dp")
    piece = lax.all_gather(images, "feat", axis=0, tiled=True)
    count = piece.shape[0]
    group = math.gcd(count, 128)
    blocks = piece.reshape(count // group, group, piece.shape[1])
    out = lax.map(lambda part: conv_pool(part, kernel, biases), blocks)
    feats = out.reshape(count, 4 * filt_count)
    width = feats.shape[1]
    residual = (
        labels[:, None] == jnp.arange(predictions.shape[1], dtype=jnp.int32)[None, :]
    ).astype(jnp.float32) - predictions
    res_upper, res_lower = split_parts(residual)
    gram = lax.psum(left_product(feats, feats), "dp")
    cross = left_product(feats, res_upper) + left_product(feats, res_lower)
    cross, gram = lax.optimization_barrier((cross, gram))
    cross = lax.psum(cross, "dp")
    gram = gram / total_images + 0.5 * jnp.eye(width, dtype=jnp.float32)
    cross = cross / total_images
    factor = jnp.linalg.cholesky(gram)
    solved = chol_solve(factor, cross)
    sol_upper, sol_lower = split_parts(solved)
    fitted = lax.psum_scatter(
        (
            jnp.dot(feats, sol_upper, preferred_element_type=jnp.float32)
            + jnp.dot(feats, sol_lower, preferred_element_type=jnp.float32)
        ).astype(jnp.bfloat16),
        "feat",
        scatter_dimension=0,
        tiled=True,
    ).astype(jnp.float32)
    mine = lax.dynamic_slice_in_dim(residual, lax.axis_index("feat") * share, share, 0)
    return (solved, mine - fitted)


def solution(mesh):
    placed = (P(("dp", "feat"), None), P("dp"), P("dp", None), P(None, "feat"), P("feat"))
    return jax.shard_map(
        shards,
        mesh=mesh,
        in_specs=placed,
        out_specs=(P("feat", None), P(("dp", "feat"), None)),
        check_vma=False,
    )
```

profile of v0, /device:TPU:0, one launch (start us, length us, event | category | flops | bytes accessed | tf_op | source)
XLA Modules:
  0.0 528.2 jit_solution(10686514619989856401)
XLA Ops:
  12.1 28.0 %all-gather.2.cloned.1.call-done = bf16[512,3072]{1,0:T(8,128)(2,1)} async-done(((bf16[64,3072]{1,0:T(8,128)(2,1)}), bf16[512,3072]{1,0:T(8,128)(2,1)}) %all-gather.2.cloned.1.call-update) | async-done | bytes 3145744 | tf_op jit(solution)/shard_map/all_gather | solution.py:52
  40.1 152.3 %while.11 = (s32[]{:T(128)}, bf16[4,128,512]{1,2,0:T(8,128)(2,1)}, bf16[4,128,3072]{2,1,0:T(8,128)(2,1)}, bf16[5,5,3,128]{3,2,1,0:T(4,128)(2,1)S(1)}, f32[128]{0:T(128)S(1)}, /*index=5*/s32[]{:T(128)}, f32[]{:T(128)}) while((s32[]{:T(128)}, bf16[4,128,512]{1,2,0:T(8,128)(2,1)}, bf16[4,128,3072]{2,1,0:T(8,128)(2,1)}, ...), condition=%wide.region_2.3_spmd, body=%wide.region_0.2_spmd.sunk | while | flops 1965359104 | bytes 109465424 | solution.py:56
  42.1 19.1 %add_maximum_fusion.2 = f32[128,28,28,128]{3,0,2,1:T(8,128)} fusion(f32[128]{0:T(128)S(1)} %get-tuple-element.169, bf16[128,32,32,3]{0,3,2,1:T(4,128)(2,1)S(1)} %reshape.101, bf16[5,5,3,128]{3,2,1,0:T(4,128)(2,1)S(1)} %get-tuple-element.168), kind=kOutput, calls=%fused_computation.clone.1 | convolution fusion | flops 1952448512 | bytes 52186368 | tf_op jit(solution)/shard_map/while/body/eval_jaxpr/conv_general_dilated | solution.py:33
  61.2 16.1 %reduce_sum.10 = f32[128,2,2,128]{3,0,2,1:T(8,128)S(1)} reduce(f32[128,2,14,2,14,128]{5,0,4,3,2,1:T(8,128)} %bitcast.85, f32[]{:T(128)} %constant.173.clone.1..sunk), dimensions={2,4}, to_apply=%region_1.1 | reduce | flops 12779520 | bytes 51642372 | tf_op jit(solution)/shard_map/while/body/eval_jaxpr/reduce_sum | solution.py:43
  80.1 19.1 %add_maximum_fusion.2 = f32[128,28,28,128]{3,0,2,1:T(8,128)} fusion(f32[128]{0:T(128)S(1)} %get-tuple-element.169, bf16[128,32,32,3]{0,3,2,1:T(4,128)(2,1)S(1)} %reshape.101, bf16[5,5,3,128]{3,2,1,0:T(4,128)(2,1)S(1)} %get-tuple-element.168), kind=kOutput, calls=%fused_computation.clone.1 | convolution fusion | flops 1952448512 | bytes 52186368 | tf_op jit(solution)/shard_map/while/body/eval_jaxpr/conv_general_dilated | solution.py:33
  99.3 16.1 %reduce_sum.10 = f32[128,2,2,128]{3,0,2,1:T(8,128)S(1)} reduce(f32[128,2,14,2,14,128]{5,0,4,3,2,1:T(8,128)} %bitcast.85, f32[]{:T(128)} %constant.173.clone.1..sunk), dimensions={2,4}, to_apply=%region_1.1 | reduce | flops 12779520 | bytes 51642372 | tf_op jit(solution)/shard_map/while/body/eval_jaxpr/reduce_sum | solution.py:43
  118.2 19.1 %add_maximum_fusion.2 = f32[128,28,28,128]{3,0,2,1:T(8,128)} fusion(f32[128]{0:T(128)S(1)} %get-tuple-element.169, bf16[128,32,32,3]{0,3,2,1:T(4,128)(2,1)S(1)} %reshape.101, bf16[5,5,3,128]{3,2,1,0:T(4,128)(2,1)S(1)} %get-tuple-element.168), kind=kOutput, calls=%fused_computation.clone.1 | convolution fusion | flops 1952448512 | bytes 52186368 | tf_op jit(solution)/shard_map/while/body/eval_jaxpr/conv_general_dilated | solution.py:33
  137.3 16.1 %reduce_sum.10 = f32[128,2,2,128]{3,0,2,1:T(8,128)S(1)} reduce(f32[128,2,14,2,14,128]{5,0,4,3,2,1:T(8,128)} %bitcast.85, f32[]{:T(128)} %constant.173.clone.1..sunk), dimensions={2,4}, to_apply=%region_1.1 | reduce | flops 12779520 | bytes 51642372 | tf_op jit(solution)/shard_map/while/body/eval_jaxpr/reduce_sum | solution.py:43
  156.3 19.1 %add_maximum_fusion.2 = f32[128,28,28,128]{3,0,2,1:T(8,128)} fusion(f32[128]{0:T(128)S(1)} %get-tuple-element.169, bf16[128,32,32,3]{0,3,2,1:T(4,128)(2,1)S(1)} %reshape.101, bf16[5,5,3,128]{3,2,1,0:T(4,128)(2,1)S(1)} %get-tuple-element.168), kind=kOutput, calls=%fused_computation.clone.1 | convolution fusion | flops 1952448512 | bytes 52186368 | tf_op jit(solution)/shard_map/while/body/eval_jaxpr/conv_general_dilated | solution.py:33
  175.4 16.1 %reduce_sum.10 = f32[128,2,2,128]{3,0,2,1:T(8,128)S(1)} reduce(f32[128,2,14,2,14,128]{5,0,4,3,2,1:T(8,128)} %bitcast.85, f32[]{:T(128)} %constant.173.clone.1..sunk), dimensions={2,4}, to_apply=%region_1.1 | reduce | flops 12779520 | bytes 51642372 | tf_op jit(solution)/shard_map/while/body/eval_jaxpr/reduce_sum | solution.py:43
  200.3 82.0 %all-reduce.4.cloned.1.call-done = f32[512,512]{1,0:T(8,128)} async-done(((f32[512,512]{1,0:T(8,128)}), f32[512,512]{1,0:T(8,128)}) %all-reduce.4.cloned.1.call-update) | async-done | bytes 1048592 | tf_op jit(solution)/shard_map/psum | solution.py:63
  290.0 11.7 %cholesky.103 = f32[128,128]{1,0:T(8,128)S(1)} custom-call(f32[128,128]{1,0:T(8,128)S(1)} %cholesky.263), custom_call_target="Cholesky" | custom-call | tf_op jit(solution)/shard_map/jit(cholesky)/cholesky | solution.py:69
  302.8 9.8 %custom-call.32 = f32[1,128,128]{1,2,0:T(8,128)S(1)} custom-call(f32[1,128,128]{2,1,0:T(8,128)S(1)} %get-tuple-element.86), custom_call_target="InvertDiagBlocksLowerTriangular" | custom-call | tf_op jit(solution)/shard_map/jit(cholesky)/cholesky | solution.py:69
  315.9 12.1 %cholesky.215 = f32[128,128]{1,0:T(8,128)S(1)} custom-call(f32[128,128]{1,0:T(8,128)S(1)} %cholesky.267), custom_call_target="Cholesky" | custom-call | tf_op jit(solution)/shard_map/jit(cholesky)/cholesky | solution.py:69
  328.6 9.8 %custom-call.33 = f32[1,128,128]{1,2,0:T(8,128)S(1)} custom-call(f32[1,128,128]{2,1,0:T(8,128)S(1)} %get-tuple-element.83), custom_call_target="InvertDiagBlocksLowerTriangular" | custom-call | tf_op jit(solution)/shard_map/jit(cholesky)/cholesky | solution.py:69
  340.8 11.7 %cholesky.236 = f32[128,128]{1,0:T(8,128)S(1)} custom-call(f32[128,128]{1,0:T(8,128)S(1)} %cholesky.272), custom_call_target="Cholesky" | custom-call | tf_op jit(solution)/shard_map/jit(cholesky)/cholesky | solution.py:69
  353.1 9.8 %custom-call.34 = f32[1,128,128]{1,2,0:T(8,128)S(1)} custom-call(f32[1,128,128]{2,1,0:T(8,128)S(1)} %get-tuple-element.80), custom_call_target="InvertDiagBlocksLowerTriangular" | custom-call | tf_op jit(solution)/shard_map/jit(cholesky)/cholesky | solution.py:69
  365.2 11.9 %cholesky.253 = f32[128,128]{1,0:T(8,128)S(1)} custom-call(f32[128,128]{1,0:T(8,128)S(1)} %convolution_subtract_fusion.6), custom_call_target="Cholesky" | custom-call | tf_op jit(solution)/shard_map/jit(cholesky)/cholesky | solution.py:69
  384.4 14.6 %while.12 = (s32[]{:T(128)}, f32[512,512]{1,0:T(8,128)}, s32[4,2]{0,1:T(2,128)S(1)}, f32[4,128,128]{2,1,0:T(8,128)}, s32[]{:T(128)}) while((s32[]{:T(128)}, f32[512,512]{1,0:T(8,128)}, s32[4,2]{0,1:T(2,128)S(1)}, f32[4,128,128]{2,1,0:T(8,128)}, s32[]{:T(128)}) %tuple.52), condition=%wide.while_cond, body=%wide.while_body.sunk | while | flops 2 | bytes 132705 | solution.py:14
  385.1 3.0 bitcast_dynamic-update-slice_fusion.2
  388.7 3.0 bitcast_dynamic-update-slice_fusion.2
  399.0 40.1 %custom-call.35 = f32[4,128,128]{1,2,0:T(8,128)S(1)} custom-call(f32[4,128,128]{2,1,0:T(8,128)} %get-tuple-element.41), custom_call_target="InvertDiagBlocksLowerTriangular" | custom-call | tf_op jit(solution)/shard_map/triangular_solve | solution.py:14
  439.1 28.5 %all-reduce.6.cloned.1.call-done = f32[512,1000]{0,1:T(8,128)} async-done(((f32[512,1000]{0,1:T(8,128)}), f32[512,1000]{0,1:T(8,128)}) %all-reduce.6.cloned.1.call-update) | async-done | bytes 2048016 | tf_op jit(solution)/shard_map/psum | solution.py:66
  488.2 31.7 %reduce-scatter.2.cloned.1.call-done = bf16[64,1000]{1,0:T(8,128)(2,1)} async-done(((bf16[512,1000]{1,0:T(8,128)(2,1)}), bf16[64,1000]{1,0:T(8,128)(2,1)}) %reduce-scatter.2.cloned.1.call-update) | async-done | bytes 128016 | tf_op jit(solution)/shard_map/reduce_scatter | solution.py:72
  (107 shorter events, 77.4 us)
Async XLA Ops:
  7.2 32.9 %all-gather.2.cloned.1.call-start = ((), (), s32[]{:S(2)}) async-start(), calls=%async_computation.1 | async-start | bytes 3538944 | tf_op jit(solution)/shard_map/all_gather | solution.py:52
  7.9 274.4 %all-reduce.4.cloned.1.call-start = ((), (), s32[]{:S(2)}) async-start(), calls=%async_computation.2 | async-start | bytes 2097152 | tf_op jit(solution)/shard_map/psum | solution.py:63
  8.7 31.4 %copy-start.5 = (f32[128]{0:T(128)S(1)}, f32[128]{0:T(128)}, u32[]{:S(2)}) copy-start(f32[128]{0:T(128)} %param.11) | copy-start | bytes 1540
  192.4 3.0 copy-start.4
  195.1 2.1 copy-start.1
  195.1 272.5 %all-reduce.6.cloned.1.call-start = ((), (), s32[]{:S(2)}) async-start(), calls=%async_computation.3 | async-start | bytes 4096000 | tf_op jit(solution)/shard_map/psum | solution.py:66
  289.0 1.0 copy-start.3
  377.1 7.3 %copy-start.6 = (s32[4]{0:T(128)S(1)}, s32[4]{0:T(128)}, u32[]{:S(2)}) copy-start(s32[4]{0:T(128)} %iota_multiply_fusion) | copy-start | bytes 52
  377.1 142.7 %reduce-scatter.2.cloned.1.call-start = ((), (), s32[]{:S(2)}) async-start(), calls=%async_computation.4 | async-start | bytes 1179648 | tf_op jit(solution)/shard_map/reduce_scatter | solution.py:72
  467.6 2.8 copy-start.2
  485.1 1.3 copy-start
Sparse Core Ops, SparseCore 0:
  9.7 30.3 all-gather.1
  195.2 86.9 all-reduce.3
  377.2 90.3 all-reduce.5
  488.3 31.4 reduce-scatter.1
where the time goes:
time: 533 us; the launch traced here: 528 us
  other arithmetic  198 us (37%)
  waiting for transfers between devices  171 us (32%)
  matrix products  108 us (20%)
  local copies, waits for them, and re-layouts  34.7 us (7%)
  between operations  16.6 us (3%)
    psum x1, waiting for transfers between devices, shards(): gram = lax.psum(left_product(feats, feats), 'dp')  82 us
    another operation x14, other arithmetic, shards(): factor = jnp.linalg.cholesky(gram)  80.7 us
    conv_general_dilated x4, matrix products, conv_pool(): lax.conv_general_dilated(pics, kernel, (1, 1), 'VALID', dimension_numbers...  76.5 us
    reduce_sum x4, other arithmetic, conv_pool(): response.reshape(count, 2, half, 2, half, filt_count).mean(axis=(2, 4))  64.5 us
    another operation x4, other arithmetic, chol_solve(): lax.linalg.triangular_solve(factor, middle, left_side=True, lower=True, t...  43.1 us
    reduce_scatter x1, waiting for transfers between devices, shards(): lax.psum_scatter((jnp.dot(feats, sol_upper, preferred_element_type=jnp.fl...  31.7 us
    psum x1, waiting for transfers between devices, shards(): cross = lax.psum(cross, 'dp')  28.5 us
    all_gather x1, waiting for transfers between devices, shards(): piece = lax.all_gather(images, 'feat', axis=0, tiled=True)  28 us
  transfers between devices with their start and end apart: 4, of which 4 were waited for; matrix products, arithmetic and copies ran while one was open for 13% of the time, Pallas kernels for 0%

commit v1 on v0

--- a/solution.py
+++ b/solution.py
@@ -45,6 +45,16 @@
 
 
 def shards(images, labels, predictions, filters, biases):
+
+    def fill_sector_up(base_x):
+        axis_id = "dp"
+        n_axis = lax.axis_size(axis_id)
+        piece_next = base_x
+        for nth in [[(k, k ^ d) for k in range(n_axis)] for d in (1, 2, 4, 8, 16) if d < n_axis]:
+            last = lax.ppermute(piece_next, axis_id, nth)
+            piece_next = piece_next + last
+        return piece_next
+
     filt_count = filters.shape[1]
     kernel = filters.reshape(KSIZE, KSIZE, CHAN, filt_count)
     share = images.shape[0]
@@ -63,7 +73,7 @@
     gram = lax.psum(left_product(feats, feats), "dp")
     cross = left_product(feats, res_upper) + left_product(feats, res_lower)
     cross, gram = lax.optimization_barrier((cross, gram))
-    cross = lax.psum(cross, "dp")
+    cross = fill_sector_up(cross)
     gram = gram / total_images + 0.5 * jnp.eye(width, dtype=jnp.float32)
     cross = cross / total_images
     factor = jnp.linalg.cholesky(gram)

time: 533 us -> 588 us (1.10)
  waiting for transfers between devices: 171 us -> 211 us
  other arithmetic: 198 us -> 209 us
    ppermute x0 -> x4, waiting for transfers between devices: none -> 67.9 us  [fill_sector_up(): last = lax.ppermute(piece_next, axis_id, nth)]
    psum x1 -> x0, waiting for transfers between devices: 28.5 us -> none  [shards(): cross = lax.psum(cross, 'dp')]
    add x0 -> x3, other arithmetic: none -> 11.2 us  [fill_sector_up(): piece_next = piece_next + last]
  transfers between devices with their start and end apart: 4 -> 7, of which waited for: 4 -> 5; matrix products, arithmetic and copies ran while one was open for 13% -> 27% of each run, Pallas kernels for 0% -> 0%
where the time goes in v1:
time: 588 us; the launch traced here: 582 us
  waiting for transfers between devices  211 us (36%)
  other arithmetic  209 us (36%)
  matrix products  108 us (18%)
  local copies, waits for them, and re-layouts  32.1 us (5%)
  between operations  16.6 us (3%)
    psum x1, waiting for transfers between devices, shards(): gram = lax.psum(left_product(feats, feats), 'dp')  82.1 us
    another operation x14, other arithmetic, shards(): factor = jnp.linalg.cholesky(gram)  80.3 us
    conv_general_dilated x4, matrix products, conv_pool(): lax.conv_general_dilated(pics, kernel, (1, 1), 'VALID', dimension_numbers...  76.5 us
    ppermute x4, waiting for transfers between devices, fill_sector_up(): last = lax.ppermute(piece_next, axis_id, nth)  67.9 us
    reduce_sum x4, other arithmetic, conv_pool(): response.reshape(count, 2, half, 2, half, filt_count).mean(axis=(2, 4))  64.5 us
    another operation x4, other arithmetic, chol_solve(): lax.linalg.triangular_solve(factor, middle, left_side=True, lower=True, t...  42.2 us
    reduce_scatter x1, waiting for transfers between devices, shards(): lax.psum_scatter((jnp.dot(feats, sol_upper, preferred_element_type=jnp.fl...  31.4 us
    all_gather x1, waiting for transfers between devices, shards(): piece = lax.all_gather(images, 'feat', axis=0, tiled=True)  28.5 us
  transfers between devices with their start and end apart: 7, of which 5 were waited for; matrix products, arithmetic and copies ran while one was open for 27% of the time, Pallas kernels for 0%

profile of v1, /device:TPU:0, one launch (start us, length us, event | category | flops | bytes accessed | tf_op | source)
XLA Modules:
  0.0 581.6 jit_solution(14744795407004950508)
XLA Ops:
  11.6 28.5 %all-gather.2.cloned.1.call-done = bf16[512,3072]{1,0:T(8,128)(2,1)} async-done(((bf16[64,3072]{1,0:T(8,128)(2,1)}), bf16[512,3072]{1,0:T(8,128)(2,1)}) %all-gather.2.cloned.1.call-update) | async-done | bytes 3145744 | tf_op jit(solution)/shard_map/all_gather | solution.py:62
  40.1 152.3 %while.11 = (s32[]{:T(128)}, bf16[4,128,512]{1,2,0:T(8,128)(2,1)}, bf16[4,128,3072]{2,1,0:T(8,128)(2,1)}, bf16[5,5,3,128]{3,2,1,0:T(4,128)(2,1)S(1)}, f32[128]{0:T(128)S(1)}, /*index=5*/s32[]{:T(128)}, f32[]{:T(128)}) while((s32[]{:T(128)}, bf16[4,128,512]{1,2,0:T(8,128)(2,1)}, bf16[4,128,3072]{2,1,0:T(8,128)(2,1)}, ...), condition=%wide.region_2.3_spmd, body=%wide.region_0.2_spmd.sunk | while | flops 1965359104 | bytes 109465424 | solution.py:66
  42.1 19.1 %add_maximum_fusion.2 = f32[128,28,28,128]{3,0,2,1:T(8,128)} fusion(f32[128]{0:T(128)S(1)} %get-tuple-element.169, bf16[128,32,32,3]{0,3,2,1:T(4,128)(2,1)S(1)} %reshape.101, bf16[5,5,3,128]{3,2,1,0:T(4,128)(2,1)S(1)} %get-tuple-element.168), kind=kOutput, calls=%fused_computation.clone.1 | convolution fusion | flops 1952448512 | bytes 52186368 | tf_op jit(solution)/shard_map/while/body/eval_jaxpr/conv_general_dilated | solution.py:33
  61.2 16.1 %reduce_sum.10 = f32[128,2,2,128]{3,0,2,1:T(8,128)S(1)} reduce(f32[128,2,14,2,14,128]{5,0,4,3,2,1:T(8,128)} %bitcast.82, f32[]{:T(128)} %constant.173.clone.1..sunk), dimensions={2,4}, to_apply=%region_1.1 | reduce | flops 12779520 | bytes 51642372 | tf_op jit(solution)/shard_map/while/body/eval_jaxpr/reduce_sum | solution.py:43
  80.1 19.1 %add_maximum_fusion.2 = f32[128,28,28,128]{3,0,2,1:T(8,128)} fusion(f32[128]{0:T(128)S(1)} %get-tuple-element.169, bf16[128,32,32,3]{0,3,2,1:T(4,128)(2,1)S(1)} %reshape.101, bf16[5,5,3,128]{3,2,1,0:T(4,128)(2,1)S(1)} %get-tuple-element.168), kind=kOutput, calls=%fused_computation.clone.1 | convolution fusion | flops 1952448512 | bytes 52186368 | tf_op jit(solution)/shard_map/while/body/eval_jaxpr/conv_general_dilated | solution.py:33
  99.3 16.1 %reduce_sum.10 = f32[128,2,2,128]{3,0,2,1:T(8,128)S(1)} reduce(f32[128,2,14,2,14,128]{5,0,4,3,2,1:T(8,128)} %bitcast.82, f32[]{:T(128)} %constant.173.clone.1..sunk), dimensions={2,4}, to_apply=%region_1.1 | reduce | flops 12779520 | bytes 51642372 | tf_op jit(solution)/shard_map/while/body/eval_jaxpr/reduce_sum | solution.py:43
  118.2 19.1 %add_maximum_fusion.2 = f32[128,28,28,128]{3,0,2,1:T(8,128)} fusion(f32[128]{0:T(128)S(1)} %get-tuple-element.169, bf16[128,32,32,3]{0,3,2,1:T(4,128)(2,1)S(1)} %reshape.101, bf16[5,5,3,128]{3,2,1,0:T(4,128)(2,1)S(1)} %get-tuple-element.168), kind=kOutput, calls=%fused_computation.clone.1 | convolution fusion | flops 1952448512 | bytes 52186368 | tf_op jit(solution)/shard_map/while/body/eval_jaxpr/conv_general_dilated | solution.py:33
  137.3 16.1 %reduce_sum.10 = f32[128,2,2,128]{3,0,2,1:T(8,128)S(1)} reduce(f32[128,2,14,2,14,128]{5,0,4,3,2,1:T(8,128)} %bitcast.82, f32[]{:T(128)} %constant.173.clone.1..sunk), dimensions={2,4}, to_apply=%region_1.1 | reduce | flops 12779520 | bytes 51642372 | tf_op jit(solution)/shard_map/while/body/eval_jaxpr/reduce_sum | solution.py:43
  156.3 19.1 %add_maximum_fusion.2 = f32[128,28,28,128]{3,0,2,1:T(8,128)} fusion(f32[128]{0:T(128)S(1)} %get-tuple-element.169, bf16[128,32,32,3]{0,3,2,1:T(4,128)(2,1)S(1)} %reshape.101, bf16[5,5,3,128]{3,2,1,0:T(4,128)(2,1)S(1)} %get-tuple-element.168), kind=kOutput, calls=%fused_computation.clone.1 | convolution fusion | flops 1952448512 | bytes 52186368 | tf_op jit(solution)/shard_map/while/body/eval_jaxpr/conv_general_dilated | solution.py:33
  175.4 16.1 %reduce_sum.10 = f32[128,2,2,128]{3,0,2,1:T(8,128)S(1)} reduce(f32[128,2,14,2,14,128]{5,0,4,3,2,1:T(8,128)} %bitcast.82, f32[]{:T(128)} %constant.173.clone.1..sunk), dimensions={2,4}, to_apply=%region_1.1 | reduce | flops 12779520 | bytes 51642372 | tf_op jit(solution)/shard_map/while/body/eval_jaxpr/reduce_sum | solution.py:43
  200.1 82.1 %all-reduce.3.cloned.1.call-done = f32[512,512]{1,0:T(8,128)} async-done(((f32[512,512]{1,0:T(8,128)}), f32[512,512]{1,0:T(8,128)}) %all-reduce.3.cloned.1.call-update) | async-done | bytes 1048592 | tf_op jit(solution)/shard_map/psum | solution.py:73
  283.1 44.1 %collective-permute-done = f32[512,1000]{0,1:T(8,128)S(1)} collective-permute-done((f32[512,1000]{0,1:T(8,128)}, f32[512,1000]{0,1:T(8,128)S(1)}, u32[]{:S(2)}, u32[]{:S(2)}) %collective-permute-start) | collective-permute-done | bytes 2048032 | tf_op jit(solution)/shard_map/ppermute | solution.py:54
  340.1 11.7 %cholesky.103 = f32[128,128]{1,0:T(8,128)S(1)} custom-call(f32[128,128]{1,0:T(8,128)S(1)} %cholesky.263), custom_call_target="Cholesky" | custom-call | tf_op jit(solution)/shard_map/jit(cholesky)/cholesky | solution.py:79
  353.0 23.8 %collective-permute-done.1 = f32[512,1000]{0,1:T(8,128)} collective-permute-done((f32[512,1000]{0,1:T(8,128)}, f32[512,1000]{0,1:T(8,128)}, u32[]{:S(2)}, u32[]{:S(2)}) %collective-permute-start.1) | collective-permute-done | bytes 2048032 | tf_op jit(solution)/shard_map/ppermute | solution.py:54
  380.9 9.8 %custom-call.32 = f32[1,128,128]{1,2,0:T(8,128)S(1)} custom-call(f32[1,128,128]{2,1,0:T(8,128)S(1)} %get-tuple-element.86), custom_call_target="InvertDiagBlocksLowerTriangular" | custom-call | tf_op jit(solution)/shard_map/jit(cholesky)/cholesky | solution.py:79
  394.0 11.7 %cholesky.215 = f32[128,128]{1,0:T(8,128)S(1)} custom-call(f32[128,128]{1,0:T(8,128)S(1)} %cholesky.267), custom_call_target="Cholesky" | custom-call | tf_op jit(solution)/shard_map/jit(cholesky)/cholesky | solution.py:79
  406.3 9.8 %custom-call.33 = f32[1,128,128]{1,2,0:T(8,128)S(1)} custom-call(f32[1,128,128]{2,1,0:T(8,128)S(1)} %get-tuple-element.83), custom_call_target="InvertDiagBlocksLowerTriangular" | custom-call | tf_op jit(solution)/shard_map/jit(cholesky)/cholesky | solution.py:79
  418.6 11.9 %cholesky.236 = f32[128,128]{1,0:T(8,128)S(1)} custom-call(f32[128,128]{1,0:T(8,128)S(1)} %cholesky.272), custom_call_target="Cholesky" | custom-call | tf_op jit(solution)/shard_map/jit(cholesky)/cholesky | solution.py:79
  431.1 9.8 %custom-call.34 = f32[1,128,128]{1,2,0:T(8,128)S(1)} custom-call(f32[1,128,128]{2,1,0:T(8,128)S(1)} %get-tuple-element.80), custom_call_target="InvertDiagBlocksLowerTriangular" | custom-call | tf_op jit(solution)/shard_map/jit(cholesky)/cholesky | solution.py:79
  443.2 11.7 %cholesky.253 = f32[128,128]{1,0:T(8,128)S(1)} custom-call(f32[128,128]{1,0:T(8,128)S(1)} %convolution_subtract_fusion.4), custom_call_target="Cholesky" | custom-call | tf_op jit(solution)/shard_map/jit(cholesky)/cholesky | solution.py:79
  456.8 4.0 add.86
  468.6 12.1 %while.12 = (s32[]{:T(128)}, f32[512,512]{1,0:T(8,128)}, s32[4,2]{0,1:T(2,128)S(1)}, f32[4,128,128]{2,1,0:T(8,128)S(1)}, s32[]{:T(128)}) while((s32[]{:T(128)}, f32[512,512]{1,0:T(8,128)}, s32[4,2]{0,1:T(2,128)S(1)}, f32[4,128,128]{2,1,0:T(8,128)S(1)}, s32[]{:T(128)}) %tuple.52), condition=%wide.while_cond, body=%wide.while_body.sunk | while | flops 2 | bytes 131181 | solution.py:14
  480.7 39.7 %custom-call.35 = f32[4,128,128]{1,2,0:T(8,128)S(1)} custom-call(f32[4,128,128]{2,1,0:T(8,128)S(1)} %get-tuple-element.41), custom_call_target="InvertDiagBlocksLowerTriangular" | custom-call | tf_op jit(solution)/shard_map/triangular_solve | solution.py:14
  541.8 31.4 %reduce-scatter.2.cloned.1.call-done = bf16[64,1000]{1,0:T(8,128)(2,1)} async-done(((bf16[512,1000]{1,0:T(8,128)(2,1)}), bf16[64,1000]{1,0:T(8,128)(2,1)}) %reduce-scatter.2.cloned.1.call-update) | async-done | bytes 128016 | tf_op jit(solution)/shard_map/reduce_scatter | solution.py:82
  (113 shorter events, 93.7 us)
Async XLA Ops:
  7.2 32.9 %all-gather.2.cloned.1.call-start = ((), (), s32[]{:S(2)}) async-start(), calls=%async_computation.1 | async-start | bytes 3538944 | tf_op jit(solution)/shard_map/all_gather | solution.py:62
  7.9 274.3 %all-reduce.3.cloned.1.call-start = ((), (), s32[]{:S(2)}) async-start(), calls=%async_computation.2 | async-start | bytes 2097152 | tf_op jit(solution)/shard_map/psum | solution.py:73
  8.7 31.4 %copy-start.5 = (f32[128]{0:T(128)S(1)}, f32[128]{0:T(128)}, u32[]{:S(2)}) copy-start(f32[128]{0:T(128)} %param.11) | copy-start | bytes 1540
  192.4 2.8 copy-start.4
  195.1 2.0 copy-start.1
  195.1 378.2 %reduce-scatter.2.cloned.1.call-start = ((), (), s32[]{:S(2)}) async-start(), calls=%async_computation.3 | async-start | bytes 1179648 | tf_op jit(solution)/shard_map/reduce_scatter | solution.py:82
  282.2 45.0 %collective-permute-start = (f32[512,1000]{0,1:T(8,128)}, f32[512,1000]{0,1:T(8,128)S(1)}, u32[]{:S(2)}, u32[]{:S(2)}) collective-permute-start(f32[512,1000]{0,1:T(8,128)} %convolution_add_fusion), channel_id=1, source_target_pairs={{0,8},{8,0},{16,24},{24,16},{32,40},{40,32},{48,56},{56,48},{64,72... | collective-permute-start | bytes 6144008 | tf_op jit(solution)/shard_map/ppermute | solution.py:54
  330.5 46.2 %collective-permute-start.1 = (f32[512,1000]{0,1:T(8,128)}, f32[512,1000]{0,1:T(8,128)}, u32[]{:S(2)}, u32[]{:S(2)}) collective-permute-start(f32[512,1000]{0,1:T(8,128)} %add.84), channel_id=1, source_target_pairs={{0,16},{8,24},{16,0},{24,8},{32,48},{40,56},{48,32},{56,40},{64,80... | collective-permute-start | bytes 6144008 | tf_op jit(solution)/shard_map/ppermute | solution.py:54
  339.1 1.0 copy-start.3
  380.7 76.1 %collective-permute-start.2 = (f32[512,1000]{0,1:T(8,128)}, f32[512,1000]{0,1:T(8,128)}, u32[]{:S(2)}, u32[]{:S(2)}) collective-permute-start(f32[512,1000]{0,1:T(8,128)} %add.85), channel_id=1, source_target_pairs={{0,32},{8,40},{16,48},{24,56},{32,0},{40,8},{48,16},{56,24},{64,96... | collective-permute-start | bytes 6144008 | tf_op jit(solution)/shard_map/ppermute | solution.py:54
  460.8 59.7 %collective-permute-start.3 = (f32[512,1000]{0,1:T(8,128)}, f32[512,1000]{0,1:T(8,128)}, u32[]{:S(2)}, u32[]{:S(2)}) collective-permute-start(f32[512,1000]{0,1:T(8,128)} %add.86), channel_id=1, source_target_pairs={{0,64},{8,72},{16,80},{24,88},{32,96},{40,104},{48,112},{56,120},{... | collective-permute-start | bytes 6144008 | tf_op jit(solution)/shard_map/ppermute | solution.py:54
  520.4 3.7 copy-start.2
  538.8 1.3 copy-start
Sparse Core Ops, SparseCore 0:
  9.7 30.3 all-gather.1
  195.2 86.9 all-reduce.2
  542.0 31.2 reduce-scatter.1
